TPU v7x, 256 devices: a whole 4x4x8 slice. The times are simulated.
256 devices in a mesh: section: 2 (over core), expert: 32 (over x, z), dp: 4 (over y).
Axes of the slice: x: 4, y: 4, z: 8, core: 2. Of those that a mesh axis runs over, the one named last changes fastest.
Arguments:
- tokens: bfloat16 [2, 16384, 1024], P(None, ('expert', 'dp')), may hold values from -6 to 6
- cotangent: bfloat16 [2, 16384, 1024], P(None, ('expert', 'dp')), may hold values from -6 to 6
- routes: int32 [2, 2, 16384, 2], P('section', None, ('expert', 'dp')), may hold values from 0 to 31, all different within a row; in each aligned block of 128 rows (0 to 127, 128 to 255, ..., all dimensions but the last counted through in order) at most 12 rows name the same one
- router: bfloat16 [2, 1024, 32], P('section'), may hold values from -0.1875 to 0.1875
- w_gate: bfloat16 [2, 32, 1024, 512], P('section', 'expert'), may hold values from -0.1875 to 0.1875
- w_up: bfloat16 [2, 32, 1024, 512], P('section', 'expert'), may hold values from -0.1875 to 0.1875
- w_down: bfloat16 [2, 32, 512, 1024], P('section', 'expert'), may hold values from -0.25 to 0.25
Outputs:
- out_layers: bfloat16 [2, 2, 16384, 1024], P('section', None, ('expert', 'dp'))
- grad_in: bfloat16 [2, 2, 16384, 1024], P('section', None, ('expert', 'dp'))
- grad_gate: float32 [2, 32, 1024, 512], P('section', 'expert', 'dp')
- grad_up: float32 [2, 32, 1024, 512], P('section', 'expert', 'dp')
- grad_down: float32 [2, 32, 512, 1024], P('section', 'expert', 'dp')
- grad_router: float32 [2, 1024, 32], P('section')
Inputs may be any that keep to these rules, and one draw needn't show every extreme that they name: `routes`: each token names 2 different experts. Within the tokens of one device (an aligned block of 128 tokens of one layer and micro-batch) no expert is named by more than 12 tokens, and in every draw some expert is named by exactly 12 tokens of some block.
All inputs are finite; a program needn't handle non-finite values.
Results may differ from a plain program's by a relative error of at most 0.012.
Values may be sent and summed in bfloat16 or wider, within the bound.
No kernel may reach another device: no remote copies, remote signals or barrier semaphores. Data moves between devices by JAX's collectives and lax.ppermute only.
A program may use at most 128 MiB of HBM per device.

v0:
```python
import math
import jax
import jax.numpy as jnp
from jax import lax
from jax.sharding import PartitionSpec as P


def from_behind(array, axis, by):
    length = lax.axis_size(axis)
    pairs = [(i, i + by) for i in range(length) if 0 <= i + by < length]
    return lax.ppermute(array, axis, pairs)


def contract_last(left, right):
    return lax.dot_general(
        left, right, (((1,), (1,)), ((), ())), preferred_element_type=jnp.float32
    )


def contract_first(left, right):
    return lax.dot_general(
        left, right, (((0,), (0,)), ((), ())), preferred_element_type=jnp.float32
    )


def slot_index(chosen, experts, capacity):
    flat = chosen.reshape(-1)
    labels = jnp.arange(experts, dtype=jnp.int32)
    onehot = (flat[:, None] == labels[None, :]).astype(jnp.int32)
    before = jnp.cumsum(onehot, axis=0) - onehot
    position = jnp.sum(before * onehot, axis=1)
    return flat * capacity + position


def route_weights(hidden, chosen, router_layer):
    logits = jnp.dot(hidden, router_layer, preferred_element_type=jnp.float32)
    labels = jnp.arange(logits.shape[1], dtype=jnp.int32)
    match = chosen[:, :, None] == labels[None, None, :]
    picked = jnp.sum(jnp.where(match, logits[:, None, :], 0.0), axis=2)
    raised = jnp.exp(picked)
    return raised / jnp.sum(raised, axis=1, keepdims=True)


def expert_trade(block):
    return lax.all_to_all(block, "expert", split_axis=0, concat_axis=0, tiled=True)


def fetch(store, place):
    return lax.dynamic_index_in_dim(store, place, 0, keepdims=False)


def store_at(store, value, place, valid):
    previous = fetch(store, place)
    return lax.dynamic_update_index_in_dim(store, jnp.where(valid, value, previous), place, 0)


def shards(tokens, cotangent, routes, router, w_gate, w_up, w_down):
    sections = lax.axis_size("section")
    sources = lax.axis_size("expert")
    groups = lax.axis_size("dp")
    section_id = lax.axis_index("section")
    batches, per_device, width = tokens.shape
    top = routes.shape[3]
    experts = router.shape[2]
    capacity = 3 * per_device * top // (2 * experts)
    router_layer = router[0]
    gate_weight = w_gate[0, 0]
    up_weight = w_up[0, 0]
    down_weight = w_down[0, 0]
    units = gate_weight.shape[1]
    total_rows = sources * capacity
    ticks = batches + sections - 1
    chosen_all = routes[0]
    labels = jnp.arange(experts, dtype=jnp.int32)
    kept_inputs = jnp.zeros((batches, per_device, width), jnp.bfloat16)
    kept_picked = jnp.zeros((batches, per_device * top, width), jnp.bfloat16)
    kept_rows = jnp.zeros((batches, total_rows, width), jnp.bfloat16)
    outputs = jnp.zeros((batches, per_device, width), jnp.bfloat16)
    carried = jnp.zeros((per_device, width), jnp.bfloat16)
    for tick in range(ticks):
        batch_index = tick - section_id
        valid = jnp.logical_and(batch_index >= 0, batch_index < batches)
        place = jnp.clip(batch_index, 0, batches - 1)
        fresh = tokens[tick] if tick < batches else jnp.zeros((per_device, width), jnp.bfloat16)
        hidden = jnp.where(section_id == 0, fresh, carried)
        chosen = fetch(chosen_all, place)
        weights = route_weights(hidden, chosen, router_layer)
        index = slot_index(chosen, experts, capacity)
        spread = (
            jnp.zeros((experts * capacity, width), jnp.bfloat16)
            .at[index]
            .set(jnp.repeat(hidden, top, axis=0))
        )
        arrived = expert_trade(spread.reshape(experts, capacity, width)).reshape(total_rows, width)
        gate = jnp.dot(arrived, gate_weight, preferred_element_type=jnp.float32)
        up_term = jnp.dot(arrived, up_weight, preferred_element_type=jnp.float32)
        inner = (jax.nn.silu(gate) * up_term).astype(jnp.bfloat16)
        produced = jnp.dot(inner, down_weight, preferred_element_type=jnp.float32).astype(
            jnp.bfloat16
        )
        returned = expert_trade(produced.reshape(sources, capacity, width)).reshape(
            experts * capacity, width
        )
        picked = returned[index]
        blended = jnp.sum(
            weights[:, :, None] * picked.reshape(per_device, top, width).astype(jnp.float32), axis=1
        )
        mixed = (hidden.astype(jnp.float32) + blended).astype(jnp.bfloat16)
        outputs = store_at(outputs, mixed, place, valid)
        kept_inputs = store_at(kept_inputs, hidden, place, valid)
        kept_picked = store_at(kept_picked, picked, place, valid)
        kept_rows = store_at(kept_rows, arrived, place, valid)
        if tick + 1 < ticks:
            carried = from_behind(mixed, "section", 1)
    kept_dgate = jnp.zeros((batches, total_rows, units), jnp.bfloat16)
    kept_dup = jnp.zeros((batches, total_rows, units), jnp.bfloat16)
    kept_inner = jnp.zeros((batches, total_rows, units), jnp.bfloat16)
    kept_grads = jnp.zeros((batches, total_rows, width), jnp.bfloat16)
    sum_router = jnp.zeros((width, experts), jnp.float32)
    grad_store = jnp.zeros((batches, per_device, width), jnp.bfloat16)
    carried = jnp.zeros((per_device, width), jnp.bfloat16)
    for tick in range(ticks):
        batch_index = tick - (sections - 1 - section_id)
        valid = jnp.logical_and(batch_index >= 0, batch_index < batches)
        place = jnp.clip(batch_index, 0, batches - 1)
        fresh = cotangent[tick] if tick < batches else jnp.zeros((per_device, width), jnp.bfloat16)
        upstream = jnp.where(section_id == sections - 1, fresh, carried)
        upstream = jnp.where(valid, upstream, jnp.zeros_like(upstream))
        chosen = fetch(chosen_all, place)
        hidden = fetch(kept_inputs, place)
        picked = fetch(kept_picked, place)
        arrived = fetch(kept_rows, place)
        weights = route_weights(hidden, chosen, router_layer)
        index = slot_index(chosen, experts, capacity)
        flowing = upstream.astype(jnp.float32)
        along = jnp.sum(
            flowing[:, None, :] * picked.reshape(per_device, top, width).astype(jnp.float32), axis=2
        )
        grad_y = (
            (weights[:, :, None] * flowing[:, None, :])
            .astype(jnp.bfloat16)
            .reshape(per_device * top, width)
        )
        spread = jnp.zeros((experts * capacity, width), jnp.bfloat16).at[index].set(grad_y)
        grad_rows = expert_trade(spread.reshape(experts, capacity, width)).reshape(
            total_rows, width
        )
        gate = jnp.dot(arrived, gate_weight, preferred_element_type=jnp.float32)
        up_term = jnp.dot(arrived, up_weight, preferred_element_type=jnp.float32)
        active = jax.nn.silu(gate)
        inner = (active * up_term).astype(jnp.bfloat16)
        d_hidden = contract_last(grad_rows, down_weight)
        sigma = jax.nn.sigmoid(gate)
        d_gate = (d_hidden * up_term * sigma * (1.0 + gate * (1.0 - sigma))).astype(jnp.bfloat16)
        d_up = (d_hidden * active).astype(jnp.bfloat16)
        d_rows = (contract_last(d_gate, gate_weight) + contract_last(d_up, up_weight)).astype(
            jnp.bfloat16
        )
        returned = expert_trade(d_rows.reshape(sources, capacity, width)).reshape(
            experts * capacity, width
        )
        back = returned[index].reshape(per_device, top, width)
        grad_h = flowing + jnp.sum(back.astype(jnp.float32), axis=1)
        grad_s = weights * (along - jnp.sum(weights * along, axis=1, keepdims=True))
        match = chosen[:, :, None] == labels[None, None, :]
        grad_logits = jnp.sum(jnp.where(match, grad_s[:, :, None], 0.0), axis=1).astype(
            jnp.bfloat16
        )
        local_router = contract_first(hidden, grad_logits)
        grad_h = grad_h + contract_last(grad_logits, router_layer)
        passed = grad_h.astype(jnp.bfloat16)
        grad_store = store_at(grad_store, passed, place, valid)
        kept_dgate = store_at(kept_dgate, d_gate, place, valid)
        kept_dup = store_at(kept_dup, d_up, place, valid)
        kept_inner = store_at(kept_inner, inner, place, valid)
        kept_grads = store_at(kept_grads, grad_rows, place, valid)
        sum_router = sum_router + local_router
        if tick + 1 < ticks:
            carried = from_behind(passed, "section", -1)
    all_rows = kept_rows.reshape(batches * total_rows, width)
    whole_gate = contract_first(all_rows, kept_dgate.reshape(batches * total_rows, units))
    whole_up = contract_first(all_rows, kept_dup.reshape(batches * total_rows, units))
    whole_down = contract_first(
        kept_inner.reshape(batches * total_rows, units),
        kept_grads.reshape(batches * total_rows, width),
    )
    shares = (
        lax.psum_scatter(
            whole_gate.astype(jnp.bfloat16), "dp", scatter_dimension=0, tiled=True
        ).astype(jnp.float32),
        lax.psum_scatter(
            whole_up.astype(jnp.bfloat16), "dp", scatter_dimension=0, tiled=True
        ).astype(jnp.float32),
        lax.psum_scatter(
            whole_down.astype(jnp.bfloat16), "dp", scatter_dimension=0, tiled=True
        ).astype(jnp.float32),
    )
    sum_gate = shares[0]
    sum_up = shares[1]
    sum_down = shares[2]
    sum_router = lax.psum(sum_router, ("expert", "dp"))
    expert_scale = 1.0 / math.sqrt(batches * groups * per_device * top)
    router_scale = 1.0 / math.sqrt(batches * per_device * sources * groups)
    return (
        outputs[None],
        grad_store[None],
        (sum_gate * expert_scale)[None, None],
        (sum_up * expert_scale)[None, None],
        (sum_down * expert_scale)[None, None],
        (sum_router * router_scale)[None],
    )


def solution(mesh):
    placed = (
        P(None, ("expert", "dp"), None),
        P(None, ("expert", "dp"), None),
        P("section", None, ("expert", "dp"), None),
        P("section", None, None),
        P("section", "expert", None, None),
        P("section", "expert", None, None),
        P("section", "expert", None, None),
    )
    return jax.shard_map(
        shards,
        mesh=mesh,
        in_specs=placed,
        out_specs=(
            P("section", None, ("expert", "dp"), None),
            P("section", None, ("expert", "dp"), None),
            P("section", "expert", "dp", None),
            P("section", "expert", "dp", None),
            P("section", "expert", "dp", None),
            P("section", None, None),
        ),
        check_vma=False,
    )
```

profile of v0, /device:TPU:2, one launch (start us, length us, event | category | flops | bytes accessed | tf_op | source)
XLA Modules:
  0.0 838.8 jit_solution(2187735484304862792)
XLA Ops:
  18.5 37.8 %all_to_all.60 = bf16[32,12,1024]{2,1,0:T(8,128)(2,1)S(1)} all-to-all(bf16[32,12,1024]{2,1,0:T(8,128)(2,1)} %reshape.769), channel_id=1, replica_groups=mesh['section'=2,'expert'=32,'dp'=4] {'expert'}, dimensions={0} | all-to-all | bytes 1572864 | tf_op jit(solution)/shard_map/all_to_all | solution.py:45
  66.7 7.7 all-to-all-start.1
  77.3 22.9 %all-to-all-done.1 = bf16[32,12,1024]{2,1,0:T(8,128)(2,1)} async-done(((bf16[32,12,1024]{2,1,0:T(8,128)(2,1)}), bf16[32,12,1024]{2,1,0:T(8,128)(2,1)}, u32[]{:S(2)}, u32[]{:S(2)}) %all-to-all-start.1) | async-done | bytes 786464 | tf_op jit(solution)/shard_map/all_to_all | solution.py:45
  102.3 3.7 gather_fusion
  127.9 7.5 all-to-all-start.2
  138.1 23.8 %all-to-all-done.2 = bf16[32,12,1024]{2,1,0:T(8,128)(2,1)} async-done(((bf16[32,12,1024]{2,1,0:T(8,128)(2,1)}), bf16[32,12,1024]{2,1,0:T(8,128)(2,1)}, u32[]{:S(2)}, u32[]{:S(2)}) %all-to-all-start.2) | async-done | bytes 786464 | tf_op jit(solution)/shard_map/all_to_all | solution.py:45
  172.2 7.8 all-to-all-start.3
  198.5 7.4 all-to-all-done.3
  230.2 7.5 all-to-all-start.4
  237.7 26.0 %all-to-all-done.4 = bf16[32,12,1024]{2,1,0:T(8,128)(2,1)} async-done(((bf16[32,12,1024]{2,1,0:T(8,128)(2,1)}), bf16[32,12,1024]{2,1,0:T(8,128)(2,1)}, u32[]{:S(2)}, u32[]{:S(2)}) %all-to-all-start.4) | async-done | bytes 786464 | tf_op jit(solution)/shard_map/all_to_all | solution.py:45
  274.1 7.6 all-to-all-start.5
  300.9 6.7 all-to-all-done.5
  327.6 7.9 all-to-all-start.6
  373.2 10.0 %all-to-all-start.7 = ((bf16[32,12,1024]{2,1,0:T(8,128)(2,1)}), bf16[32,12,1024]{2,1,0:T(8,128)(2,1)}, u32[]{:S(2)}, u32[]{:S(2)}) async-start(bf16[32,12,1024]{2,1,0:T(8,128)(2,1)} %reshape.790), calls=%async_computation.7 | async-start | bytes 2097152 | tf_op jit(solution)/shard_map/all_to_all | solution.py:45
  398.0 9.3 %all-to-all-done.7 = bf16[32,12,1024]{2,1,0:T(8,128)(2,1)} async-done(((bf16[32,12,1024]{2,1,0:T(8,128)(2,1)}), bf16[32,12,1024]{2,1,0:T(8,128)(2,1)}, u32[]{:S(2)}, u32[]{:S(2)}) %all-to-all-start.7) | async-done | bytes 786464 | tf_op jit(solution)/shard_map/all_to_all | solution.py:45
  444.4 7.6 all-to-all-start.8
  481.4 4.0 fusion.94
  489.6 9.5 %all-to-all-start.9 = ((bf16[32,12,1024]{2,1,0:T(8,128)(2,1)}), bf16[32,12,1024]{2,1,0:T(8,128)(2,1)}, u32[]{:S(2)}, u32[]{:S(2)}) async-start(bf16[32,12,1024]{2,1,0:T(8,128)(2,1)} %reshape.795), calls=%async_computation.9 | async-start | bytes 2097152 | tf_op jit(solution)/shard_map/all_to_all | solution.py:45
  511.6 14.2 %all-to-all-done.9 = bf16[32,12,1024]{2,1,0:T(8,128)(2,1)} async-done(((bf16[32,12,1024]{2,1,0:T(8,128)(2,1)}), bf16[32,12,1024]{2,1,0:T(8,128)(2,1)}, u32[]{:S(2)}, u32[]{:S(2)}) %all-to-all-start.9) | async-done | bytes 786464 | tf_op jit(solution)/shard_map/all_to_all | solution.py:45
  527.9 3.7 gather_fusion.4
  564.3 7.8 all-to-all-start.10
  601.4 4.2 fusion.93
  632.3 9.8 %all-to-all-start.11 = ((bf16[32,12,1024]{2,1,0:T(8,128)(2,1)}), bf16[32,12,1024]{2,1,0:T(8,128)(2,1)}, u32[]{:S(2)}, u32[]{:S(2)}) async-start(bf16[32,12,1024]{2,1,0:T(8,128)(2,1)} %reshape.800), calls=%async_computation.11 | async-start | bytes 2097152 | tf_op jit(solution)/shard_map/all_to_all | solution.py:45
  653.2 162.6 %all-reduce.2.cloned.1.call-done = f32[1024,32]{0,1:T(8,128)} async-done(((f32[1024,32]{0,1:T(8,128)}), f32[1024,32]{0,1:T(8,128)}) %all-reduce.2.cloned.1.call-update) | async-done | bytes 131088 | tf_op jit(solution)/shard_map/psum | solution.py:201
  (420 shorter events, 404.7 us)
Async XLA Ops:
  8.0 53.1 %copy-start = (bf16[1,1,512,1024]{3,2,1,0:T(8,128)(2,1)S(1)}, bf16[1,1,512,1024]{3,2,1,0:T(8,128)(2,1)}, u32[]{:S(2)}) copy-start(bf16[1,1,512,1024]{3,2,1,0:T(8,128)(2,1)} %param.13) | copy-start | bytes 3145732
  9.5 125.8 %copy-start.35 = (s32[1,1,128,2]{2,3,1,0:T(2,128)}, s32[1,1,128,2]{2,3,1,0:T(2,128)S(1)}, u32[]{:S(2)}) copy-start(s32[1,1,128,2]{2,3,1,0:T(2,128)S(1)} %get-tuple-element.57) | copy-start | bytes 3076
  9.5 290.2 %copy-start.32 = (s32[1,1,128,2]{2,3,1,0:T(2,128)}, s32[1,1,128,2]{2,3,1,0:T(2,128)S(1)}, u32[]{:S(2)}) copy-start(s32[1,1,128,2]{2,3,1,0:T(2,128)S(1)} %get-tuple-element.55) | copy-start | bytes 3076
  66.7 33.5 %all-to-all-start.1 = ((bf16[32,12,1024]{2,1,0:T(8,128)(2,1)}), bf16[32,12,1024]{2,1,0:T(8,128)(2,1)}, u32[]{:S(2)}, u32[]{:S(2)}) async-start(bf16[32,12,1024]{2,1,0:T(8,128)(2,1)} %reshape.771), calls=%async_computation.1 | async-start | bytes 2097152 | tf_op jit(solution)/shard_map/all_to_all | solution.py:45
  112.9 2.8 collective-permute-start
  127.9 34.1 %all-to-all-start.2 = ((bf16[32,12,1024]{2,1,0:T(8,128)(2,1)}), bf16[32,12,1024]{2,1,0:T(8,128)(2,1)}, u32[]{:S(2)}, u32[]{:S(2)}) async-start(bf16[32,12,1024]{2,1,0:T(8,128)(2,1)} %reshape.775), calls=%async_computation.2 | async-start | bytes 2097152 | tf_op jit(solution)/shard_map/all_to_all | solution.py:45
  172.2 33.7 %all-to-all-start.3 = ((bf16[32,12,1024]{2,1,0:T(8,128)(2,1)}), bf16[32,12,1024]{2,1,0:T(8,128)(2,1)}, u32[]{:S(2)}, u32[]{:S(2)}) async-start(bf16[32,12,1024]{2,1,0:T(8,128)(2,1)} %reshape.777), calls=%async_computation.3 | async-start | bytes 2097152 | tf_op jit(solution)/shard_map/all_to_all | solution.py:45
  217.9 3.1 collective-permute-start.1
  230.2 33.6 %all-to-all-start.4 = ((bf16[32,12,1024]{2,1,0:T(8,128)(2,1)}), bf16[32,12,1024]{2,1,0:T(8,128)(2,1)}, u32[]{:S(2)}, u32[]{:S(2)}) async-start(bf16[32,12,1024]{2,1,0:T(8,128)(2,1)} %reshape.781), calls=%async_computation.4 | async-start | bytes 2097152 | tf_op jit(solution)/shard_map/all_to_all | solution.py:45
  274.1 33.5 %all-to-all-start.5 = ((bf16[32,12,1024]{2,1,0:T(8,128)(2,1)}), bf16[32,12,1024]{2,1,0:T(8,128)(2,1)}, u32[]{:S(2)}, u32[]{:S(2)}) async-start(bf16[32,12,1024]{2,1,0:T(8,128)(2,1)} %reshape.783), calls=%async_computation.5 | async-start | bytes 2097152 | tf_op jit(solution)/shard_map/all_to_all | solution.py:45
  327.6 35.5 %all-to-all-start.6 = ((bf16[32,12,1024]{2,1,0:T(8,128)(2,1)}), bf16[32,12,1024]{2,1,0:T(8,128)(2,1)}, u32[]{:S(2)}, u32[]{:S(2)}) async-start(bf16[32,12,1024]{2,1,0:T(8,128)(2,1)} %reshape.786), calls=%async_computation.6 | async-start | bytes 2097152 | tf_op jit(solution)/shard_map/all_to_all | solution.py:45
  373.2 34.1 %all-to-all-start.7 = ((bf16[32,12,1024]{2,1,0:T(8,128)(2,1)}), bf16[32,12,1024]{2,1,0:T(8,128)(2,1)}, u32[]{:S(2)}, u32[]{:S(2)}) async-start(bf16[32,12,1024]{2,1,0:T(8,128)(2,1)} %reshape.790), calls=%async_computation.7 | async-start | bytes 2097152 | tf_op jit(solution)/shard_map/all_to_all | solution.py:45
  420.6 3.5 collective-permute-start.2
  444.4 34.8 %all-to-all-start.8 = ((bf16[32,12,1024]{2,1,0:T(8,128)(2,1)}), bf16[32,12,1024]{2,1,0:T(8,128)(2,1)}, u32[]{:S(2)}, u32[]{:S(2)}) async-start(bf16[32,12,1024]{2,1,0:T(8,128)(2,1)} %reshape.793), calls=%async_computation.8 | async-start | bytes 2097152 | tf_op jit(solution)/shard_map/all_to_all | solution.py:45
  453.2 45.9 %copy-start.44 = (f32[128,2]{0,1:T(2,128)}, f32[128,2]{0,1:T(2,128)S(1)}, u32[]{:S(2)}) copy-start(f32[128,2]{0,1:T(2,128)S(1)} %select_reduce_fusion.1) | copy-start | bytes 3076
  489.6 36.1 %all-to-all-start.9 = ((bf16[32,12,1024]{2,1,0:T(8,128)(2,1)}), bf16[32,12,1024]{2,1,0:T(8,128)(2,1)}, u32[]{:S(2)}, u32[]{:S(2)}) async-start(bf16[32,12,1024]{2,1,0:T(8,128)(2,1)} %reshape.795), calls=%async_computation.9 | async-start | bytes 2097152 | tf_op jit(solution)/shard_map/all_to_all | solution.py:45
  539.9 7.4 collective-permute-start.3
  564.3 35.0 %all-to-all-start.10 = ((bf16[32,12,1024]{2,1,0:T(8,128)(2,1)}), bf16[32,12,1024]{2,1,0:T(8,128)(2,1)}, u32[]{:S(2)}, u32[]{:S(2)}) async-start(bf16[32,12,1024]{2,1,0:T(8,128)(2,1)} %reshape.798), calls=%async_computation.10 | async-start | bytes 2097152 | tf_op jit(solution)/shard_map/all_to_all | solution.py:45
  572.1 243.8 %all-reduce.2.cloned.1.call-start = ((), (), s32[]{:S(2)}) async-start(), calls=%async_computation.18 | async-start | bytes 262144 | tf_op jit(solution)/shard_map/psum | solution.py:201
  599.0 226.4 %reduce-scatter.8.cloned.1.call-start = ((), (), s32[]{:S(2)}) async-start(), calls=%async_computation.17 | async-start | bytes 1310720 | tf_op jit(solution)/shard_map/reduce_scatter | solution.py:194
  617.5 209.9 %reduce-scatter.6.cloned.1.call-start = ((), (), s32[]{:S(2)}) async-start(), calls=%async_computation.16 | async-start | bytes 1310720 | tf_op jit(solution)/shard_map/reduce_scatter | solution.py:191
  632.3 185.2 %all-to-all-start.11 = ((bf16[32,12,1024]{2,1,0:T(8,128)(2,1)}), bf16[32,12,1024]{2,1,0:T(8,128)(2,1)}, u32[]{:S(2)}, u32[]{:S(2)}) async-start(bf16[32,12,1024]{2,1,0:T(8,128)(2,1)} %reshape.800), calls=%async_computation.11 | async-start | bytes 2097152 | tf_op jit(solution)/shard_map/all_to_all | solution.py:45
  642.1 187.0 %reduce-scatter.4.cloned.1.call-start = ((), (), s32[]{:S(2)}) async-start(), calls=%async_computation.15 | async-start | bytes 1310720 | tf_op jit(solution)/shard_map/reduce_scatter | solution.py:188
  652.4 165.0 %copy-start.26 = (bf16[1,2,128,1024]{3,2,1,0:T(8,128)(2,1)}, bf16[1,2,128,1024]{3,2,1,0:T(8,128)(2,1)S(1)}, u32[]{:S(2)}) copy-start(bf16[1,2,128,1024]{3,2,1,0:T(8,128)(2,1)S(1)} %fusion.109) | copy-start | bytes 1572868
  (49 other events, 314.7 us)
Sparse Core Ops, SparseCore 0:
  599.1 216.7 all-reduce.1
Sparse Core Ops, SparseCore 1:
  617.5 27.5 reduce-scatter.7
  647.6 25.9 reduce-scatter.5
  675.9 26.1 reduce-scatter.3
where the time goes:
time: 853 us; the launch traced here: 839 us
  waiting for transfers between devices  274 us (32%)
  local copies, waits for them, and re-layouts  234 us (27%)
  other arithmetic  102 us (12%)
  starting transfers between devices  97.7 us (11%)
  matrix products  76.8 us (9%)
  blocking collectives  37.8 us (4%)
  between operations  16.9 us (2%)
    psum x1, waiting for transfers between devices, shards(): sum_router = lax.psum(sum_router, ('expert', 'dp'))  163 us
    all_to_all x11, waiting for transfers between devices, expert_trade(): lax.all_to_all(block, 'expert', split_axis=0, concat_axis=0, tiled=True)  111 us
    all_to_all x11, starting transfers between devices, expert_trade(): lax.all_to_all(block, 'expert', split_axis=0, concat_axis=0, tiled=True)  90.7 us
    all_to_all x1, blocking collectives, expert_trade(): lax.all_to_all(block, 'expert', split_axis=0, concat_axis=0, tiled=True)  37.8 us
    dynamic_slice x22, local copies, waits for them, and re-layouts, fetch(): return lax.dynamic_index_in_dim(store, place, 0, keepdims=False)  25.3 us
    dot_general x12, matrix products, contract_last(): lax.dot_general(left, right, (((1,), (1,)), ((), ())), preferred_element_...  23.4 us
    dynamic_update_slice x12, other arithmetic, store_at(): lax.dynamic_update_index_in_dim(store, jnp.where(valid, value, previous),...  22.2 us
    mul x9, local copies, waits for them, and re-layouts, shards(): weights[:, :, None] * flowing[:, None, :]  21.8 us
  transfers between devices with their start and end apart: 19, of which 9 were waited for; matrix products, arithmetic and copies ran while one was open for 26% of the time, Pallas kernels for 0%

commit v1 on v0

--- a/solution.py
+++ b/solution.py
@@ -198,7 +198,7 @@
     sum_gate = shares[0]
     sum_up = shares[1]
     sum_down = shares[2]
-    sum_router = lax.psum(sum_router, ("expert", "dp"))
+    sum_router = jnp.sum(lax.all_gather(sum_router, ("expert", "dp")), axis=0)
     expert_scale = 1.0 / math.sqrt(batches * groups * per_device * top)
     router_scale = 1.0 / math.sqrt(batches * per_device * sources * groups)
     return (

time: 853 us -> 843 us (0.988)
  waiting for transfers between devices: 274 us -> 231 us
  blocking collectives: 37.8 us -> 71.4 us
  starting transfers between devices: 97.7 us -> 86.3 us
    psum x1 -> x0, waiting for transfers between devices: 163 us -> none  [shards(): sum_router = lax.psum(sum_router, ('expert', 'dp'))]
    all_gather x0 -> x1, waiting for transfers between devices: none -> 102 us  [shards(): sum_router = jnp.sum(lax.all_gather(sum_router, ('expert', 'dp')), axis=0)]
    all_to_all x1 -> x2, blocking collectives: 37.8 us -> 71.4 us  [expert_trade(): lax.all_to_all(block, 'expert', split_axis=0, concat_axis=0, tiled=True)]
    all_to_all x11 -> x10, waiting for transfers between devices: 111 us -> 129 us  [expert_trade(): lax.all_to_all(block, 'expert', split_axis=0, concat_axis=0, tiled=True)]
    unnamed x110 -> x99, local copies, waits for them, and re-layouts: 10 us -> 26.5 us
    all_to_all x11 -> x10, starting transfers between devices: 90.7 us -> 80 us  [expert_trade(): lax.all_to_all(block, 'expert', split_axis=0, concat_axis=0, tiled=True)]
  transfers between devices with their start and end apart: 19 -> 18, of which waited for: 9 -> 13; matrix products, arithmetic and copies ran while one was open for 26% -> 23% of each run, Pallas kernels for 0% -> 0%
where the time goes in v1:
time: 843 us; the launch traced here: 828 us
  local copies, waits for them, and re-layouts  242 us (29%)
  waiting for transfers between devices  231 us (27%)
  other arithmetic  106 us (13%)
  starting transfers between devices  86.3 us (10%)
  matrix products  74.5 us (9%)
  blocking collectives  71.4 us (8%)
  between operations  16.4 us (2%)
    all_to_all x10, waiting for transfers between devices, expert_trade(): lax.all_to_all(block, 'expert', split_axis=0, concat_axis=0, tiled=True)  129 us
    all_gather x1, waiting for transfers between devices, shards(): sum_router = jnp.sum(lax.all_gather(sum_router, ('expert', 'dp')), axis=0)  102 us
    all_to_all x10, starting transfers between devices, expert_trade(): lax.all_to_all(block, 'expert', split_axis=0, concat_axis=0, tiled=True)  80 us
    all_to_all x2, blocking collectives, expert_trade(): lax.all_to_all(block, 'expert', split_axis=0, concat_axis=0, tiled=True)  71.4 us
    unnamed x99, local copies, waits for them, and re-layouts  26.5 us
    dynamic_slice x22, local copies, waits for them, and re-layouts, fetch(): return lax.dynamic_index_in_dim(store, place, 0, keepdims=False)  25.3 us
    dynamic_update_slice x12, other arithmetic, store_at(): lax.dynamic_update_index_in_dim(store, jnp.where(valid, value, previous),...  22.3 us
    dot_general x12, matrix products, contract_last(): lax.dot_general(left, right, (((1,), (1,)), ((), ())), preferred_element_...  22.2 us
  transfers between devices with their start and end apart: 18, of which 13 were waited for; matrix products, arithmetic and copies ran while one was open for 23% of the time, Pallas kernels for 0%

profile of v1, /device:TPU:2, one launch (start us, length us, event | category | flops | bytes accessed | tf_op | source)
XLA Modules:
  0.0 828.1 jit_solution(5291505058692671329)
XLA Ops:
  18.6 37.8 %all_to_all.60 = bf16[32,12,1024]{2,1,0:T(8,128)(2,1)S(1)} all-to-all(bf16[32,12,1024]{2,1,0:T(8,128)(2,1)} %reshape.778), channel_id=1, replica_groups=mesh['section'=2,'expert'=32,'dp'=4] {'expert'}, dimensions={0} | all-to-all | bytes 1572864 | tf_op jit(solution)/shard_map/all_to_all | solution.py:45
  66.7 7.7 all-to-all-start.1
  77.3 22.9 %all-to-all-done.1 = bf16[32,12,1024]{2,1,0:T(8,128)(2,1)} async-done(((bf16[32,12,1024]{2,1,0:T(8,128)(2,1)}), bf16[32,12,1024]{2,1,0:T(8,128)(2,1)}, u32[]{:S(2)}, u32[]{:S(2)}) %all-to-all-start.1) | async-done | bytes 786464 | tf_op jit(solution)/shard_map/all_to_all | solution.py:45
  127.9 7.5 all-to-all-start.2
  139.3 22.7 %all-to-all-done.2 = bf16[32,12,1024]{2,1,0:T(8,128)(2,1)} async-done(((bf16[32,12,1024]{2,1,0:T(8,128)(2,1)}), bf16[32,12,1024]{2,1,0:T(8,128)(2,1)}, u32[]{:S(2)}, u32[]{:S(2)}) %all-to-all-start.2) | async-done | bytes 786464 | tf_op jit(solution)/shard_map/all_to_all | solution.py:45
  172.3 7.7 all-to-all-start.3
  195.7 10.3 %all-to-all-done.3 = bf16[32,12,1024]{2,1,0:T(8,128)(2,1)} async-done(((bf16[32,12,1024]{2,1,0:T(8,128)(2,1)}), bf16[32,12,1024]{2,1,0:T(8,128)(2,1)}, u32[]{:S(2)}, u32[]{:S(2)}) %all-to-all-start.3) | async-done | bytes 786464 | tf_op jit(solution)/shard_map/all_to_all | solution.py:45
  230.2 33.6 %all_to_all.61 = bf16[32,12,1024]{2,1,0:T(8,128)(2,1)} all-to-all(bf16[32,12,1024]{2,1,0:T(8,128)(2,1)} %reshape.790), channel_id=1, replica_groups=mesh['section'=2,'expert'=32,'dp'=4] {'expert'}, dimensions={0} | all-to-all | bytes 1572864 | tf_op jit(solution)/shard_map/all_to_all | solution.py:45
  274.0 7.6 all-to-all-start.5
  297.0 10.5 %all-to-all-done.5 = bf16[32,12,1024]{2,1,0:T(8,128)(2,1)} async-done(((bf16[32,12,1024]{2,1,0:T(8,128)(2,1)}), bf16[32,12,1024]{2,1,0:T(8,128)(2,1)}, u32[]{:S(2)}, u32[]{:S(2)}) %all-to-all-start.5) | async-done | bytes 786464 | tf_op jit(solution)/shard_map/all_to_all | solution.py:45
  324.6 8.1 all-to-all-start.6
  353.6 4.7 all-to-all-done.6
  368.2 7.4 all-to-all-start.7
  384.1 17.4 %all-to-all-done.7 = bf16[32,12,1024]{2,1,0:T(8,128)(2,1)} async-done(((bf16[32,12,1024]{2,1,0:T(8,128)(2,1)}), bf16[32,12,1024]{2,1,0:T(8,128)(2,1)}, u32[]{:S(2)}, u32[]{:S(2)}) %all-to-all-start.7) | async-done | bytes 786464 | tf_op jit(solution)/shard_map/all_to_all | solution.py:45
  436.6 7.5 all-to-all-start.8
  481.5 8.6 %all-to-all-start.9 = ((bf16[32,12,1024]{2,1,0:T(8,128)(2,1)}), bf16[32,12,1024]{2,1,0:T(8,128)(2,1)}, u32[]{:S(2)}, u32[]{:S(2)}) async-start(bf16[32,12,1024]{2,1,0:T(8,128)(2,1)} %reshape.804), calls=%async_computation.9 | async-start | bytes 2097152 | tf_op jit(solution)/shard_map/all_to_all | solution.py:45
  499.1 17.5 %all-to-all-done.9 = bf16[32,12,1024]{2,1,0:T(8,128)(2,1)} async-done(((bf16[32,12,1024]{2,1,0:T(8,128)(2,1)}), bf16[32,12,1024]{2,1,0:T(8,128)(2,1)}, u32[]{:S(2)}, u32[]{:S(2)}) %all-to-all-start.9) | async-done | bytes 786464 | tf_op jit(solution)/shard_map/all_to_all | solution.py:45
  554.1 7.6 all-to-all-start.10
  591.8 4.3 fusion.93
  640.6 10.3 %all-to-all-start.11 = ((bf16[32,12,1024]{2,1,0:T(8,128)(2,1)}), bf16[32,12,1024]{2,1,0:T(8,128)(2,1)}, u32[]{:S(2)}, u32[]{:S(2)}) async-start(bf16[32,12,1024]{2,1,0:T(8,128)(2,1)} %reshape.809), calls=%async_computation.11 | async-start | bytes 2097152 | tf_op jit(solution)/shard_map/all_to_all | solution.py:45
  658.7 21.3 %all-to-all-done.11 = bf16[32,12,1024]{2,1,0:T(8,128)(2,1)} async-done(((bf16[32,12,1024]{2,1,0:T(8,128)(2,1)}), bf16[32,12,1024]{2,1,0:T(8,128)(2,1)}, u32[]{:S(2)}, u32[]{:S(2)}) %all-to-all-start.11) | async-done | bytes 786464 | tf_op jit(solution)/shard_map/all_to_all | solution.py:45
  692.6 101.8 %all-gather.3.cloned.1.call-done = f32[131072,32]{0,1:T(8,128)} async-done(((f32[1024,32]{0,1:T(8,128)}), f32[131072,32]{0,1:T(8,128)}) %all-gather.3.cloned.1.call-update) | async-done | bytes 16777232 | tf_op jit(solution)/shard_map/all_gather | solution.py:201
  794.3 17.7 %copy.158 = f32[4,8,128,1024]{3,2,1,0:T(8,128)} copy(f32[4,8,128,1024]{3,1,2,0:T(8,128)} %bitcast.446) | data formatting | bytes 33554432
  812.0 8.1 bitcast_reduce_fusion
  (409 shorter events, 401.3 us)
Async XLA Ops:
  8.0 53.2 %copy-start = (bf16[1,1,512,1024]{3,2,1,0:T(8,128)(2,1)S(1)}, bf16[1,1,512,1024]{3,2,1,0:T(8,128)(2,1)}, u32[]{:S(2)}) copy-start(bf16[1,1,512,1024]{3,2,1,0:T(8,128)(2,1)} %param.13) | copy-start | bytes 3145732
  9.5 172.6 %copy-start.35 = (s32[1,1,128,2]{2,3,1,0:T(2,128)}, s32[1,1,128,2]{2,3,1,0:T(2,128)S(1)}, u32[]{:S(2)}) copy-start(s32[1,1,128,2]{2,3,1,0:T(2,128)S(1)} %get-tuple-element.57) | copy-start | bytes 3076
  9.6 286.8 %copy-start.32 = (s32[1,1,128,2]{2,3,1,0:T(2,128)}, s32[1,1,128,2]{2,3,1,0:T(2,128)S(1)}, u32[]{:S(2)}) copy-start(s32[1,1,128,2]{2,3,1,0:T(2,128)S(1)} %get-tuple-element.55) | copy-start | bytes 3076
  9.6 407.7 %copy-start.31 = (s32[1,1,128,2]{2,3,1,0:T(2,128)}, s32[1,1,128,2]{2,3,1,0:T(2,128)S(1)}, u32[]{:S(2)}) copy-start(s32[1,1,128,2]{2,3,1,0:T(2,128)S(1)} %get-tuple-element.63) | copy-start | bytes 3076
  9.6 480.5 %copy-start.28 = (s32[1,1,128,2]{2,3,1,0:T(2,128)}, s32[1,1,128,2]{2,3,1,0:T(2,128)S(1)}, u32[]{:S(2)}) copy-start(s32[1,1,128,2]{2,3,1,0:T(2,128)S(1)} %get-tuple-element.21) | copy-start | bytes 3076
  66.7 33.5 %all-to-all-start.1 = ((bf16[32,12,1024]{2,1,0:T(8,128)(2,1)}), bf16[32,12,1024]{2,1,0:T(8,128)(2,1)}, u32[]{:S(2)}, u32[]{:S(2)}) async-start(bf16[32,12,1024]{2,1,0:T(8,128)(2,1)} %reshape.780), calls=%async_computation.1 | async-start | bytes 2097152 | tf_op jit(solution)/shard_map/all_to_all | solution.py:45
  113.0 2.6 collective-permute-start
  127.9 34.2 %all-to-all-start.2 = ((bf16[32,12,1024]{2,1,0:T(8,128)(2,1)}), bf16[32,12,1024]{2,1,0:T(8,128)(2,1)}, u32[]{:S(2)}, u32[]{:S(2)}) async-start(bf16[32,12,1024]{2,1,0:T(8,128)(2,1)} %reshape.784), calls=%async_computation.2 | async-start | bytes 2097152 | tf_op jit(solution)/shard_map/all_to_all | solution.py:45
  172.3 33.7 %all-to-all-start.3 = ((bf16[32,12,1024]{2,1,0:T(8,128)(2,1)}), bf16[32,12,1024]{2,1,0:T(8,128)(2,1)}, u32[]{:S(2)}, u32[]{:S(2)}) async-start(bf16[32,12,1024]{2,1,0:T(8,128)(2,1)} %reshape.786), calls=%async_computation.3 | async-start | bytes 2097152 | tf_op jit(solution)/shard_map/all_to_all | solution.py:45
  217.9 3.1 collective-permute-start.1
  274.0 33.5 %all-to-all-start.5 = ((bf16[32,12,1024]{2,1,0:T(8,128)(2,1)}), bf16[32,12,1024]{2,1,0:T(8,128)(2,1)}, u32[]{:S(2)}, u32[]{:S(2)}) async-start(bf16[32,12,1024]{2,1,0:T(8,128)(2,1)} %reshape.792), calls=%async_computation.5 | async-start | bytes 2097152 | tf_op jit(solution)/shard_map/all_to_all | solution.py:45
  324.6 33.7 %all-to-all-start.6 = ((bf16[32,12,1024]{2,1,0:T(8,128)(2,1)}), bf16[32,12,1024]{2,1,0:T(8,128)(2,1)}, u32[]{:S(2)}, u32[]{:S(2)}) async-start(bf16[32,12,1024]{2,1,0:T(8,128)(2,1)} %reshape.795), calls=%async_computation.6 | async-start | bytes 2097152 | tf_op jit(solution)/shard_map/all_to_all | solution.py:45
  368.2 33.3 %all-to-all-start.7 = ((bf16[32,12,1024]{2,1,0:T(8,128)(2,1)}), bf16[32,12,1024]{2,1,0:T(8,128)(2,1)}, u32[]{:S(2)}, u32[]{:S(2)}) async-start(bf16[32,12,1024]{2,1,0:T(8,128)(2,1)} %reshape.799), calls=%async_computation.7 | async-start | bytes 2097152 | tf_op jit(solution)/shard_map/all_to_all | solution.py:45
  414.6 3.4 collective-permute-start.2
  436.6 34.5 %all-to-all-start.8 = ((bf16[32,12,1024]{2,1,0:T(8,128)(2,1)}), bf16[32,12,1024]{2,1,0:T(8,128)(2,1)}, u32[]{:S(2)}, u32[]{:S(2)}) async-start(bf16[32,12,1024]{2,1,0:T(8,128)(2,1)} %reshape.802), calls=%async_computation.8 | async-start | bytes 2097152 | tf_op jit(solution)/shard_map/all_to_all | solution.py:45
  481.5 35.1 %all-to-all-start.9 = ((bf16[32,12,1024]{2,1,0:T(8,128)(2,1)}), bf16[32,12,1024]{2,1,0:T(8,128)(2,1)}, u32[]{:S(2)}, u32[]{:S(2)}) async-start(bf16[32,12,1024]{2,1,0:T(8,128)(2,1)} %reshape.804), calls=%async_computation.9 | async-start | bytes 2097152 | tf_op jit(solution)/shard_map/all_to_all | solution.py:45
  530.5 3.4 collective-permute-start.3
  554.1 35.6 %all-to-all-start.10 = ((bf16[32,12,1024]{2,1,0:T(8,128)(2,1)}), bf16[32,12,1024]{2,1,0:T(8,128)(2,1)}, u32[]{:S(2)}, u32[]{:S(2)}) async-start(bf16[32,12,1024]{2,1,0:T(8,128)(2,1)} %reshape.807), calls=%async_computation.10 | async-start | bytes 2097152 | tf_op jit(solution)/shard_map/all_to_all | solution.py:45
  561.8 125.2 %reduce-scatter.4.cloned.1.call-start = ((), (), s32[]{:S(2)}) async-start(), calls=%async_computation.15 | async-start | bytes 1310720 | tf_op jit(solution)/shard_map/reduce_scatter | solution.py:188
  603.5 85.5 %reduce-scatter.6.cloned.1.call-start = ((), (), s32[]{:S(2)}) async-start(), calls=%async_computation.16 | async-start | bytes 1310720 | tf_op jit(solution)/shard_map/reduce_scatter | solution.py:191
  610.9 79.8 %reduce-scatter.8.cloned.1.call-start = ((), (), s32[]{:S(2)}) async-start(), calls=%async_computation.17 | async-start | bytes 1310720 | tf_op jit(solution)/shard_map/reduce_scatter | solution.py:194
  633.0 161.3 %all-gather.3.cloned.1.call-start = ((), (), s32[]{:S(2)}) async-start(), calls=%async_computation.18 | async-start | bytes 16908288 | tf_op jit(solution)/shard_map/all_gather | solution.py:201
  640.6 39.3 %all-to-all-start.11 = ((bf16[32,12,1024]{2,1,0:T(8,128)(2,1)}), bf16[32,12,1024]{2,1,0:T(8,128)(2,1)}, u32[]{:S(2)}, u32[]{:S(2)}) async-start(bf16[32,12,1024]{2,1,0:T(8,128)(2,1)} %reshape.809), calls=%async_computation.11 | async-start | bytes 2097152 | tf_op jit(solution)/shard_map/all_to_all | solution.py:45
  686.9 125.1 %copy-start.24 = (bf16[1,2,128,1024]{3,2,1,0:T(8,128)(2,1)}, bf16[1,2,128,1024]{3,2,1,0:T(8,128)(2,1)S(1)}, u32[]{:S(2)}) copy-start(bf16[1,2,128,1024]{3,2,1,0:T(8,128)(2,1)S(1)} %fusion.112) | copy-start | bytes 1572868
  (42 other events, 265.6 us)
Sparse Core Ops, SparseCore 0:
  603.6 27.3 reduce-scatter.3
  633.6 26.0 reduce-scatter.5
  662.2 26.0 reduce-scatter.7
Sparse Core Ops, SparseCore 1:
  637.7 156.6 all-gather.2
